TPU v7x, 32 devices: a whole 2x2x4 slice. The times are simulated.
32 devices in a mesh: seq: 16 (over z, y, x), tp: 2 (over core).
Axes of the slice: x: 2, y: 2, z: 4, core: 2. Of those that a mesh axis runs over, the one named last changes fastest.
Arguments:
- prefill_hidden: bfloat16 [2048, 5120], P('seq', 'tp'), may hold values from -14 to 14
- prefill_query_rows: bfloat16 [2048, 5120], P('seq', 'tp'), may hold values from -250 to 250
- prefill_key_value: bfloat16 [2, 2048, 1024], P(None, 'seq', 'tp'), may hold values from -5 to 5
- request_prefix_cache: bfloat16 [2, 16, 768, 1024], P(None, 'seq', None, 'tp'), may hold values from -5 to 5
- prefix_lengths: int32 [16], replicated, may hold values from 0 to 768, as said below
- decode_hidden: bfloat16 [4, 5120], P(None, 'tp'), may hold values from -14 to 14
- decode_query_rows: bfloat16 [4, 5120], P(None, 'tp'), may hold values from -250 to 250
- decode_kv: bfloat16 [2, 4, 1024], P(None, None, 'tp'), may hold values from -5 to 5
- decode_slot_cache: bfloat16 [2, 5, 2048, 1024], P(None, None, 'seq', 'tp'), may hold values from -5 to 5
- cache_lengths: int32 [4], replicated, may hold values from 512 to 2048, as said below
- slot_table: int32 [4], replicated, may hold values from 0 to 4, as said below
- out_weight: bfloat16 [5120, 5120], P('tp', 'seq'), may hold values from -0.078125 to 0.078125
- final_gain: bfloat16 [5120], replicated, may hold values from 0.5 to 1.5
- head_weight: bfloat16 [5120, 152064], P(None, ('seq', 'tp')), may hold values from -4 to 4
Outputs:
- prefill_out: bfloat16 [2048, 5120], P('seq', 'tp')
- decode_out: bfloat16 [4, 5120], P(None, 'tp')
- log_probs: float32 [20, 152064], P(None, ('seq', 'tp'))
Inputs may be any that keep to these rules, and one draw needn't show every extreme that they name: `prefix_lengths`: some request has no cached prefix and some has exactly 768 cached tokens. `cache_lengths`: some request has exactly 2048 cached tokens. `slot_table`: distinct slots.
All inputs are finite; a program needn't handle non-finite values.
Results may differ from a plain program's by a relative error of at most 0.0035.
Values may be sent and summed in bfloat16 or wider, within the bound.
No kernel may reach another device: no remote copies, remote signals or barrier semaphores. Data moves between devices by JAX's collectives and lax.ppermute only.
A program may use at most 128 MiB of HBM per device.

v0:
```python
import math
import jax
import jax.numpy as jnp
from jax import lax
from jax.sharding import PartitionSpec as P

QUERY_HEADS = 40
KEY_HEADS = 8
HEAD_SIZE = 128
neg_large = -1e30
exact = lax.Precision.HIGHEST
norm_eps = 1e-06


def merged(value, axis, join):
    pieces = jax.tree.map(lambda part: lax.all_gather(part, axis), value)
    head = jax.tree.map(lambda part: part[0], pieces)
    tail = jax.tree.map(lambda part: part[1:], pieces)
    subtotal, _ = lax.scan(lambda subtotal, piece: (join(subtotal, piece), None), head, tail)
    return subtotal


def join_parts(earlier, later):
    row_max = jnp.maximum(earlier[0], later[0])
    factor_one = jnp.exp(earlier[0] - row_max)
    factor_two = jnp.exp(later[0] - row_max)
    return (
        row_max,
        earlier[1] * factor_one + later[1] * factor_two,
        earlier[2] * factor_one[..., None] + later[2] * factor_two[..., None],
    )


def join_totals(earlier, later):
    row_max = jnp.maximum(earlier[0], later[0])
    return (
        row_max,
        earlier[1] * jnp.exp(earlier[0] - row_max) + later[1] * jnp.exp(later[0] - row_max),
    )


def local(
    prefill_hidden,
    prefill_query_rows,
    prefill_key_value,
    request_prefix_cache,
    prefix_lengths,
    decode_hidden,
    decode_query_rows,
    decode_kv,
    decode_slot_cache,
    cache_lengths,
    slot_table,
    out_weight,
    final_gain,
    head_weight,
):
    query_group_width = QUERY_HEADS // KEY_HEADS
    score_scale = 1.0 / math.sqrt(HEAD_SIZE)
    kv_local = prefill_key_value.shape[2] // HEAD_SIZE
    seq_index = lax.axis_index("seq")
    span_len = prefill_query_rows.shape[0]
    prefix_len = request_prefix_cache.shape[2]
    prefix_end = lax.dynamic_slice_in_dim(prefix_lengths, seq_index, 1)[0]
    query_matrix = prefill_query_rows.reshape(span_len, kv_local, query_group_width, HEAD_SIZE)
    joined_keys = jnp.concatenate([request_prefix_cache[0, 0], prefill_key_value[0]], 0).reshape(
        prefix_len + span_len, kv_local, HEAD_SIZE
    )
    value_matrix = jnp.concatenate([request_prefix_cache[1, 0], prefill_key_value[1]], 0).reshape(
        prefix_len + span_len, kv_local, HEAD_SIZE
    )
    key_place = jnp.arange(prefix_len + span_len)
    query_place = jnp.arange(span_len)
    live_mask = jnp.where(
        key_place[None, :] < prefix_len,
        key_place[None, :] < prefix_end,
        key_place[None, :] - prefix_len <= query_place[:, None],
    )
    scores = (
        jnp.einsum("rkgh,skh->kgrs", query_matrix, joined_keys, preferred_element_type=jnp.float32)
        * score_scale
    )
    masked = jnp.where(live_mask, scores, neg_large)
    row_max = jnp.max(masked, axis=-1, keepdims=True)
    weights = jnp.where(live_mask, jnp.exp(masked - row_max), 0.0)
    row_sum = jnp.sum(weights, axis=-1)
    weights_low = weights.astype(jnp.bfloat16)
    mixed = jnp.einsum(
        "kgrs,skh->rkgh", weights_low, value_matrix, preferred_element_type=jnp.float32
    )
    prefill_attention = (
        (mixed / jnp.transpose(row_sum, (2, 0, 1))[..., None])
        .astype(jnp.bfloat16)
        .reshape(span_len, -1)
    )
    decode_count = decode_query_rows.shape[0]
    ctx_local = decode_slot_cache.shape[2]
    chosen = jnp.take(decode_slot_cache, slot_table, axis=1)
    positions = seq_index * ctx_local + jnp.arange(ctx_local)
    decode_live = (positions[None, :] < cache_lengths[:, None])[:, None, None, :]
    decode_token_rows = decode_query_rows.reshape(
        decode_count, kv_local, query_group_width, HEAD_SIZE
    )
    cache_keys = chosen[0].reshape(decode_count, ctx_local, kv_local, HEAD_SIZE)
    cache_values = chosen[1].reshape(decode_count, ctx_local, kv_local, HEAD_SIZE)
    decode_scores = (
        jnp.einsum(
            "bkgh,bskh->bkgs", decode_token_rows, cache_keys, preferred_element_type=jnp.float32
        )
        * score_scale
    )
    decode_masked = jnp.where(decode_live, decode_scores, neg_large)
    decode_max = jnp.max(decode_masked, axis=-1)
    decode_weights = jnp.where(decode_live, jnp.exp(decode_masked - decode_max[..., None]), 0.0)
    decode_sum = jnp.sum(decode_weights, axis=-1)
    decode_mixed = jnp.einsum(
        "bkgs,bskh->bkgh", decode_weights, cache_values.astype(jnp.float32), precision=exact
    )
    best = lax.pmax(decode_max, "seq")
    factors = jnp.exp(decode_max - best)
    totals, mixtures = lax.psum((decode_sum * factors, decode_mixed * factors[..., None]), "seq")
    combined = (best, totals, mixtures)
    own_keys = decode_kv[0].reshape(decode_count, kv_local, HEAD_SIZE)
    own_values = decode_kv[1].reshape(decode_count, kv_local, HEAD_SIZE).astype(jnp.float32)
    own_scores = (
        jnp.einsum("bkgh,bkh->bkg", decode_token_rows, own_keys, preferred_element_type=jnp.float32)
        * score_scale
    )
    own_mixed = jnp.broadcast_to(own_values[:, :, None, :], combined[2].shape)
    final_max, final_sum, final_mixed = join_parts(
        combined, (own_scores, jnp.ones_like(own_scores), own_mixed)
    )
    decode_attention = (
        (final_mixed / final_sum[..., None]).astype(jnp.bfloat16).reshape(decode_count, -1)
    )
    attention_all = jnp.concatenate([prefill_attention, decode_attention], 0)
    every_row = lax.all_gather(attention_all, "seq", axis=0, tiled=True)
    column_block = jnp.dot(every_row, out_weight, preferred_element_type=jnp.float32)
    partial_terms = lax.all_to_all(column_block, "seq", split_axis=0, concat_axis=1, tiled=True)
    summed = lax.psum_scatter(partial_terms, "tp", scatter_dimension=1, tiled=True)
    residual = jnp.concatenate([prefill_hidden, decode_hidden], 0).astype(jnp.float32)
    updated = (residual + summed).astype(jnp.bfloat16)
    prefill_out = updated[:span_len]
    decode_out = updated[span_len:]
    gathered = lax.all_gather(prefill_out[span_len - 1 :], ("seq", "tp"), axis=0, tiled=True)
    decode_full = lax.all_gather(decode_out, "tp", axis=1, tiled=True)
    n_seq = lax.axis_size("seq")
    n_tp = lax.axis_size("tp")
    feature_width = prefill_out.shape[1]
    prefill_full = gathered.reshape(n_seq, n_tp * feature_width)
    head_input = jnp.concatenate([decode_full, prefill_full], 0).astype(jnp.float32)
    mean_square = jnp.mean(head_input * head_input, axis=-1, keepdims=True)
    normed = (
        head_input * lax.rsqrt(mean_square + norm_eps) * final_gain.astype(jnp.float32)
    ).astype(jnp.bfloat16)
    logits = jnp.dot(normed, head_weight, preferred_element_type=jnp.float32)
    local_max = jnp.max(logits, axis=-1)
    local_sum = jnp.sum(jnp.exp(logits - local_max[:, None]), axis=-1)
    global_max, global_sum = merged((local_max, local_sum), ("seq", "tp"), join_totals)
    log_probs = logits - (global_max + jnp.log(global_sum))[:, None]
    return (prefill_out, decode_out, log_probs)


def solution(mesh):
    return jax.shard_map(
        local,
        mesh=mesh,
        in_specs=(
            P("seq", "tp"),
            P("seq", "tp"),
            P(None, "seq", "tp"),
            P(None, "seq", None, "tp"),
            P(),
            P(None, "tp"),
            P(None, "tp"),
            P(None, None, "tp"),
            P(None, None, "seq", "tp"),
            P(),
            P(),
            P("tp", "seq"),
            P(),
            P(None, ("seq", "tp")),
        ),
        out_specs=(P("seq", "tp"), P(None, "tp"), P(None, ("seq", "tp"))),
        check_vma=False,
    )
```

profile of v0, /device:TPU:10, one launch (start us, length us, event | category | flops | bytes accessed | tf_op | source)
XLA Modules:
  0.0 531.2 jit_solution(17046051987952885032)
XLA Ops:
  7.2 0.8 compare_select_fusion
  8.0 0.7 compare_and_fusion
  8.7 1.9 gather_fusion
  10.9 0.3 copy.61
  11.3 0.3 fusion.58
  11.7 31.6 %pmax.7 = f32[4,4,5]{2,1,0:T(4,128)S(1)} all-reduce(f32[4,4,5]{2,1,0:T(4,128)S(1)} %get-tuple-element.62), channel_id=1, replica_groups=mesh['seq'=16,'tp'=2] {'seq'}, use_global_device_ids=true, to_apply=%region_3.4 | all-reduce | flops 80 | bytes 640 | tf_op jit(solution)/shard_map/pmax | solution.py:119
  43.2 0.2 fusion.36
  43.4 0.3 copy.63
  43.9 1.0 convolution_multiply_fusion.1
  44.9 74.1 %all-reduce.3 = (f32[4,4,5,128]{3,2,1,0:T(8,128)S(1)}, f32[4,4,5]{2,1,0:T(4,128)S(1)}) all-reduce(f32[4,4,5,128]{3,2,1,0:T(8,128)S(1)} %convolution_multiply_fusion.1, f32[4,4,5]{2,1,0:T(4,128)S(1)} %bitcast.100), channel_id=1, replica_groups=mesh['seq'=16,'tp'=2] {'seq'}, use_global_device_ids=true, to_apply=%region_4.5 | all-reduce | flops 10320 | bytes 82560 | tf_op jit(solution)/shard_map/psum | solution.py:121
  119.1 0.6 dynamic_slice.10
  119.7 0.6 iota_compare_fusion.1
  120.4 2.4 fusion.55
  122.7 1.4 copy.77
  124.1 1.2 copy.56
  125.3 1.7 fusion.57
  127.0 1.0 copy.78
  128.0 0.8 copy.57
  128.8 2.2 copy.58
  131.0 1.2 copy.52
  132.2 0.8 copy.53
  132.9 1.4 fusion.31
  134.3 7.4 %fusion.59 = (f32[4,5,128]{2,1,0:T(8,128)S(1)}, bf16[4,5,128,896]{2,3,1,0:T(8,128)(2,1)}) fusion(pred[128,896]{0,1:T(8,128)(4,1)} %fusion.31, bf16[128,4,5,128]{0,3,2,1:T(8,128)(2,1)} %bitcast.92, bf16[128,4,128]{2,0,1:T(8,128)(2,1)S(1)} %copy-done.5, bf16[768,4,128]{2,0,1:T(8,128)(2,1)S(1)} %copy-done.2), kind=kOutput, calls=%fused_computation.82 | convolution fusion | flops 602801024 | bytes 6285312 | tf_op jit(solution)/shard_map/sub | solution.py:85
  141.8 4.1 fusion.18
  145.9 1.3 copy.65
  147.2 0.9 maximum_bitcast_fusion.3
  148.2 0.2 reduce-scatter.2.cloned.1.call-start
  148.4 143.1 %all-gather.6.cloned.1.call-done = bf16[16,132,2560]{2,1,0:T(8,128)(2,1)} async-done(((bf16[1,132,2560]{2,1,0:T(8,128)(2,1)}), bf16[16,132,2560]{2,1,0:T(8,128)(2,1)}) %all-gather.6.cloned.1.call-update) | async-done | bytes 10813456 | tf_op jit(solution)/shard_map/all_gather | solution.py:137
  291.5 11.0 %reshape.134 = bf16[2112,2560]{1,0:T(8,128)(2,1)} reshape(bf16[16,132,2560]{2,1,0:T(8,128)(2,1)} %all-gather.6.cloned.1.call-done) | data formatting | bytes 21626880
  302.5 10.3 %fusion.62 = f32[2112,320]{1,0:T(8,128)} fusion(bf16[2112,2560]{1,0:T(8,128)(2,1)} %reshape.134, bf16[2560,320]{0,1:T(8,128)(2,1)S(1)} %copy-done), kind=kOutput, calls=%fused_computation.85 | convolution fusion | flops 3460300800 | bytes 15155200 | tf_op jit(solution)/shard_map/dot_general | solution.py:138
  312.8 4.2 all_to_all.14
  317.0 80.1 %all_to_all.19 = f32[16,132,320]{2,1,0:T(8,128)S(1)} all-to-all(f32[16,132,320]{2,1,0:T(8,128)} %all_to_all.14), channel_id=1, replica_groups=mesh['seq'=16,'tp'=2] {'seq'}, dimensions={0} | all-to-all | bytes 5406720 | tf_op jit(solution)/shard_map/all_to_all | solution.py:139
  397.1 2.3 copy.67
  399.4 4.8 all_to_all.17
  404.2 10.2 %reduce-scatter.2.cloned.1.call-done = f32[132,2560]{1,0:T(8,128)} async-done(((f32[132,5120]{1,0:T(8,128)}), f32[132,2560]{1,0:T(8,128)}) %reduce-scatter.2.cloned.1.call-update) | async-done | bytes 1351696 | tf_op jit(solution)/shard_map/reduce_scatter | solution.py:140
  414.4 1.5 add_convert_fusion
  415.9 31.5 %all-gather.3 = bf16[32,1,2560]{2,1,0:T(2,128)(2,1)S(1)} all-gather(bf16[1,1,2560]{2,1,0:T(2,128)(2,1)S(1)} %slice_bitcast_fusion), channel_id=1, replica_groups=mesh['seq'=16,'tp'=2] {'seq','tp'}, dimensions={0}, use_global_device_ids=true | all-gather | bytes 168960 | tf_op jit(solution)/shard_map/all_gather | solution.py:145
  447.4 0.9 reduce
  448.4 1.8 all_gather.22
  450.3 0.2 fusion.28
  450.5 19.8 %fusion.60 = (f32[20]{0:T(128)S(1)}, f32[20,4752]{1,0:T(8,128)S(1)}) fusion(bf16[5120,4752]{0,1:T(8,128)(2,1)} %param.29, f32[5120]{0:T(1024)S(1)} %convert_element_type.43, f32[20]{0:T(128)S(1)} %add_rsqrt_fusion, bf16[16,5120]{1,0:T(8,128)(2,1)S(1)} %reshape.110, bf16[4,5120]{1,0:T(4,128)(2,1)S(1)} %all_gather.22), kind=kOutput, calls=%fused_computation.83 | convolution fusion | flops 974021440 | bytes 49266080 | tf_op jit(solution)/shard_map/dot_general | solution.py:156
  470.3 0.3 exponential_reduce_fusion
  470.6 0.2 dynamic-update-slice
  470.8 0.2 dynamic-update-slice.1
  471.0 49.9 %all-reduce.2 = (f32[640]{0:T(1024)S(1)}, f32[640]{0:T(1024)S(1)}) all-reduce(f32[640]{0:T(1024)S(1)} %dynamic-update-slice, f32[640]{0:T(1024)S(1)} %dynamic-update-slice.1), channel_id=2, replica_groups=mesh['seq'=16,'tp'=2] {'seq','tp'}, use_global_device_ids=true, to_apply=%add | all-reduce | flops 1280 | bytes 10240
  521.1 0.9 slice.69
  522.2 1.3 while.12
  523.5 0.9 broadcast_subtract_fusion
  (91 shorter events, 2.2 us)
Async XLA Ops:
  7.2 295.3 %copy-start = (bf16[2560,320]{0,1:T(8,128)(2,1)S(1)}, bf16[2560,320]{0,1:T(8,128)(2,1)}, u32[]{:S(2)}) copy-start(bf16[2560,320]{0,1:T(8,128)(2,1)} %param.27) | copy-start | bytes 4915204
  7.2 284.3 %all-gather.6.cloned.1.call-start = ((), (), s32[]{:S(2)}) async-start(), calls=%async_computation.3 | async-start | bytes 11837440 | tf_op jit(solution)/shard_map/all_gather | solution.py:137
  8.7 2.5 copy-start.9
  8.7 2.6 copy-start.12
  10.7 33.1 %copy-start.11 = (bf16[2,4,512]{2,1,0:T(4,128)(2,1)S(1)}, bf16[2,4,512]{2,1,0:T(4,128)(2,1)}, u32[]{:S(2)}) copy-start(bf16[2,4,512]{2,1,0:T(4,128)(2,1)} %param.23) | copy-start | bytes 24580
  10.8 108.3 %copy-start.13 = (s32[16]{0:T(128)S(1)}, s32[16]{0:T(128)}, u32[]{:S(2)}) copy-start(s32[16]{0:T(128)} %param.20) | copy-start | bytes 196
  125.3 9.0 %copy-start.2 = (bf16[768,4,128]{2,0,1:T(8,128)(2,1)S(1)}, bf16[768,4,128]{2,0,1:T(8,128)(2,1)}, u32[]{:S(2)}) copy-start(bf16[768,4,128]{2,0,1:T(8,128)(2,1)} %copy.56) | copy-start | bytes 2359300
  128.8 5.5 %copy-start.5 = (bf16[128,4,128]{2,0,1:T(8,128)(2,1)S(1)}, bf16[128,4,128]{2,0,1:T(8,128)(2,1)}, u32[]{:S(2)}) copy-start(bf16[128,4,128]{2,0,1:T(8,128)(2,1)} %copy.57) | copy-start | bytes 393220
  134.3 7.5 %copy-start.3 = (bf16[1,1,768,512]{2,3,1,0:T(8,128)(2,1)S(1)}, bf16[1,1,768,512]{2,3,1,0:T(8,128)(2,1)}, u32[]{:S(2)}) copy-start(bf16[1,1,768,512]{2,3,1,0:T(8,128)(2,1)} %copy.52) | copy-start | bytes 2359300
  134.3 7.5 %copy-start.6 = (bf16[1,128,512]{1,2,0:T(8,128)(2,1)S(1)}, bf16[1,128,512]{1,2,0:T(8,128)(2,1)}, u32[]{:S(2)}) copy-start(bf16[1,128,512]{1,2,0:T(8,128)(2,1)} %copy.53) | copy-start | bytes 393220
  148.2 266.2 %reduce-scatter.2.cloned.1.call-start = ((), (), s32[]{:S(2)}) async-start(), calls=%async_computation.2 | async-start | bytes 4177920 | tf_op jit(solution)/shard_map/reduce_scatter | solution.py:140
  399.4 4.8 copy-start.10
  399.4 15.0 %copy-start.4 = (bf16[128,2560]{1,0:T(8,128)(2,1)S(1)}, bf16[128,2560]{1,0:T(8,128)(2,1)}, u32[]{:S(2)}) copy-start(bf16[128,2560]{1,0:T(8,128)(2,1)} %param.16) | copy-start | bytes 1966084
  399.4 15.0 %copy-start.8 = (bf16[4,2560]{1,0:T(4,128)(2,1)S(1)}, bf16[4,2560]{1,0:T(4,128)(2,1)}, u32[]{:S(2)}) copy-start(bf16[4,2560]{1,0:T(4,128)(2,1)} %param.21) | copy-start | bytes 61444
  415.9 54.4 %copy-start.7 = (bf16[4,2560]{1,0:T(4,128)(2,1)}, bf16[4,2560]{1,0:T(4,128)(2,1)S(1)}, u32[]{:S(2)}) copy-start(bf16[4,2560]{1,0:T(4,128)(2,1)S(1)} %slice.70) | copy-start | bytes 61444
  450.5 73.9 %copy-start.1 = (bf16[2560,320]{0,1:T(8,128)(2,1)S(1)}, bf16[2560,320]{0,1:T(8,128)(2,1)}, u32[]{:S(2)}) copy-start(bf16[2560,320]{0,1:T(8,128)(2,1)} %param.27) | copy-start | bytes 4915204
Sparse Core Ops, SparseCore 0:
  148.3 143.1 all-gather.5
  404.3 10.0 reduce-scatter.1
where the time goes:
time: 532 us; the launch traced here: 531 us
  blocking collectives  269 us (51%)
  waiting for transfers between devices  153 us (29%)
  matrix products  43.1 us (8%)
  local copies, waits for them, and re-layouts  41.2 us (8%)
  between operations  14.4 us (3%)
  other arithmetic  9.66 us (2%)
    all_gather x1, waiting for transfers between devices, local(): every_row = lax.all_gather(attention_all, 'seq', axis=0, tiled=True)  143 us
    all_to_all x1, blocking collectives, local(): lax.all_to_all(column_block, 'seq', split_axis=0, concat_axis=1, tiled=True)  80.1 us
    psum x1, blocking collectives, local(): lax.psum((decode_sum * factors, decode_mixed * factors[..., None]), 'seq')  74.1 us
    unnamed x1, blocking collectives  49.9 us
    pmax x1, blocking collectives, local(): best = lax.pmax(decode_max, 'seq')  31.6 us
    all_gather x1, blocking collectives, local(): lax.all_gather(prefill_out[span_len - 1:], ('seq', 'tp'), axis=0, tiled=T...  31.5 us
    dot_general x1, matrix products, local(): logits = jnp.dot(normed, head_weight, preferred_element_type=jnp.float32)  19.8 us
    unnamed x37, local copies, waits for them, and re-layouts  16.2 us
  transfers between devices with their start and end apart: 2, of which 2 were waited for; matrix products, arithmetic and copies ran while one was open for 0% of the time, Pallas kernels for 0%

commit v1 on v0

--- a/solution.py
+++ b/solution.py
@@ -10,6 +10,28 @@
 neg_large = -1e30
 exact = lax.Precision.HIGHEST
 norm_eps = 1e-06
+
+
+def cut_along(array, dim, size):
+    before, after = (array.shape[:dim], array.shape[dim + 1 :])
+    return jnp.moveaxis(array.reshape(*before, size, -1, *after), dim, 0)
+
+
+def joined_along(parts, dim):
+    parts = jnp.moveaxis(parts, 0, dim)
+    shape = parts.shape
+    return parts.reshape(*shape[:dim], shape[dim] * shape[dim + 1], *shape[dim + 2 :])
+
+
+def exchange_in_pairs(shard, axis, split_dim, concat_dim):
+    size, place = (lax.axis_size(axis), lax.axis_index(axis))
+    tiles = cut_along(shard, split_dim, size)
+    gathered = [tiles[place]]
+    for lap in range(1, size):
+        sent = tiles[place ^ lap]
+        gathered.append(lax.ppermute(sent, axis, [(i, i ^ lap) for i in range(size)]))
+    tiles = jnp.stack(gathered)[place ^ jnp.arange(size)]
+    return joined_along(tiles, concat_dim)
 
 
 def merged(value, axis, join):
@@ -136,7 +158,7 @@
     attention_all = jnp.concatenate([prefill_attention, decode_attention], 0)
     every_row = lax.all_gather(attention_all, "seq", axis=0, tiled=True)
     column_block = jnp.dot(every_row, out_weight, preferred_element_type=jnp.float32)
-    partial_terms = lax.all_to_all(column_block, "seq", split_axis=0, concat_axis=1, tiled=True)
+    partial_terms = exchange_in_pairs(column_block, "seq", 0, 1)
     summed = lax.psum_scatter(partial_terms, "tp", scatter_dimension=1, tiled=True)
     residual = jnp.concatenate([prefill_hidden, decode_hidden], 0).astype(jnp.float32)
     updated = (residual + summed).astype(jnp.bfloat16)

time: 532 us -> 553 us (1.039)
  blocking collectives: 269 us -> 189 us
  waiting for transfers between devices: 153 us -> 205 us
  starting transfers between devices: 0.26 us -> 30.2 us
  local copies, waits for them, and re-layouts: 41.2 us -> 61.8 us
    all_to_all x1 -> x0, blocking collectives: 80.1 us -> none  [local(): lax.all_to_all(column_block, 'seq', split_axis=0, concat_axis=1, tiled=True)]
    ppermute x0 -> x15, waiting for transfers between devices: none -> 49.1 us  [exchange_in_pairs(): lax.ppermute(sent, axis, [(i, i ^ lap) for i in range(size)])]
    ppermute x0 -> x15, starting transfers between devices: none -> 29.9 us  [exchange_in_pairs(): lax.ppermute(sent, axis, [(i, i ^ lap) for i in range(size)])]
    all_to_all x3 -> x0, local copies, waits for them, and re-layouts: 11.2 us -> none  [local(): lax.all_to_all(column_block, 'seq', split_axis=0, concat_axis=1, tiled=True)]
    unnamed x37 -> x45, local copies, waits for them, and re-layouts: 16.2 us -> 26 us
    reshape x0 -> x2, local copies, waits for them, and re-layouts: none -> 8.97 us  [the longest x1 4.74 us: joined_along(): parts.reshape(*shape[:dim], shape[dim] * shape[dim + 1], *shape[dim + 2:])]
  transfers between devices with their start and end apart: 2 -> 17, of which waited for: 2 -> 13; matrix products, arithmetic and copies ran while one was open for 0% -> 2% of each run, Pallas kernels for 0% -> 0%
where the time goes in v1:
time: 553 us; the launch traced here: 552 us
  waiting for transfers between devices  205 us (37%)
  blocking collectives  189 us (34%)
  local copies, waits for them, and re-layouts  61.8 us (11%)
  matrix products  42.1 us (8%)
  starting transfers between devices  30.2 us (5%)
  between operations  14.5 us (3%)
  other arithmetic  9.08 us (2%)
    all_gather x1, waiting for transfers between devices, local(): every_row = lax.all_gather(attention_all, 'seq', axis=0, tiled=True)  143 us
    psum x1, blocking collectives, local(): lax.psum((decode_sum * factors, decode_mixed * factors[..., None]), 'seq')  74 us
    unnamed x1, blocking collectives  49.9 us
    ppermute x15, waiting for transfers between devices, exchange_in_pairs(): lax.ppermute(sent, axis, [(i, i ^ lap) for i in range(size)])  49.1 us
    pmax x1, blocking collectives, local(): best = lax.pmax(decode_max, 'seq')  31.6 us
    all_gather x1, blocking collectives, local(): lax.all_gather(prefill_out[span_len - 1:], ('seq', 'tp'), axis=0, tiled=T...  31.5 us
    ppermute x15, starting transfers between devices, exchange_in_pairs(): lax.ppermute(sent, axis, [(i, i ^ lap) for i in range(size)])  29.9 us
    unnamed x45, local copies, waits for them, and re-layouts  26 us
  transfers between devices with their start and end apart: 17, of which 13 were waited for; matrix products, arithmetic and copies ran while one was open for 2% of the time, Pallas kernels for 0%

profile of v1, /device:TPU:10, one launch (start us, length us, event | category | flops | bytes accessed | tf_op | source)
XLA Modules:
  0.0 551.6 jit_solution(16229846985475379854)
XLA Ops:
  8.7 1.2 dynamic_slice.58
  10.6 2.4 fusion.56
  12.9 1.4 copy.77
  14.3 1.2 copy.56
  15.5 1.7 fusion.58
  19.0 2.2 copy.58
  21.2 1.2 copy.52
  23.3 7.4 %fusion.60 = (f32[4,5,128]{2,1,0:T(8,128)S(1)}, bf16[4,5,128,896]{2,3,1,0:T(8,128)(2,1)}) fusion(pred[128,896]{0,1:T(8,128)(4,1)S(1)} %fusion.31, bf16[128,4,5,128]{0,3,2,1:T(8,128)(2,1)} %bitcast.154, bf16[128,4,128]{2,0,1:T(8,128)(2,1)} %copy.57, bf16[768,4,128]{2,0,1:T(8,128)(2,1)S(1)} %copy-done.2), kind=kOutput, calls=%fused_computation.117 | convolution fusion | flops 602801024 | bytes 6285312 | tf_op jit(solution)/shard_map/sub | solution.py:107
  30.7 3.3 fusion.18
  34.3 1.9 gather_fusion
  37.3 1.3 copy.61
  39.1 31.6 %pmax.7 = f32[4,4,5]{2,1,0:T(4,128)S(1)} all-reduce(f32[4,4,5]{2,1,0:T(4,128)S(1)} %get-tuple-element.78), channel_id=1, replica_groups=mesh['seq'=16,'tp'=2] {'seq'}, use_global_device_ids=true, to_apply=%region_3.4 | all-reduce | flops 80 | bytes 640 | tf_op jit(solution)/shard_map/pmax | solution.py:141
  72.3 74.0 %all-reduce.3 = (f32[4,4,5,128]{3,2,1,0:T(8,128)S(1)}, f32[4,4,5]{2,1,0:T(4,128)S(1)}) all-reduce(f32[4,4,5,128]{3,2,1,0:T(8,128)S(1)} %convolution_multiply_fusion.1, f32[4,4,5]{2,1,0:T(4,128)S(1)} %bitcast.162), channel_id=1, replica_groups=mesh['seq'=16,'tp'=2] {'seq'}, use_global_device_ids=true, to_apply=%region_4.5 | all-reduce | flops 10320 | bytes 82560 | tf_op jit(solution)/shard_map/psum | solution.py:143
  147.8 143.0 %all-gather.6.cloned.1.call-done = bf16[16,132,2560]{2,1,0:T(8,128)(2,1)} async-done(((bf16[1,132,2560]{2,1,0:T(8,128)(2,1)}), bf16[16,132,2560]{2,1,0:T(8,128)(2,1)}) %all-gather.6.cloned.1.call-update) | async-done | bytes 10813456 | tf_op jit(solution)/shard_map/all_gather | solution.py:159
  290.8 11.0 %reshape.163 = bf16[2112,2560]{1,0:T(8,128)(2,1)} reshape(bf16[16,132,2560]{2,1,0:T(8,128)(2,1)} %all-gather.6.cloned.1.call-done) | data formatting | bytes 21626880
  301.8 10.3 %fusion.63 = f32[2112,320]{1,0:T(8,128)} fusion(bf16[2112,2560]{1,0:T(8,128)(2,1)} %reshape.163, bf16[2560,320]{0,1:T(8,128)(2,1)S(1)} %copy-done), kind=kOutput, calls=%fused_computation.120 | convolution fusion | flops 3460300800 | bytes 15155200 | tf_op jit(solution)/shard_map/dot_general | solution.py:160
  312.0 4.2 reshape.129
  316.3 2.9 dynamic-slice_bitcast_fusion
  319.9 1.5 collective-permute-start.1
  321.5 1.3 collective-permute-start.2
  322.7 2.1 collective-permute-start.3
  325.0 3.8 collective-permute-done
  328.8 1.9 collective-permute-start.5
  331.4 1.9 collective-permute-start.6
  334.0 2.2 collective-permute-start.7
  336.9 1.8 collective-permute-start.8
  340.1 1.6 collective-permute-start.9
  342.4 4.1 collective-permute-done.5
  348.7 4.1 collective-permute-start.11
  353.5 15.2 %collective-permute-done.7 = f32[132,320]{1,0:T(8,128)S(1)} collective-permute-done((f32[132,320]{1,0:T(8,128)S(1)}, f32[132,320]{1,0:T(8,128)S(1)}, u32[]{:S(2)}, u32[]{:S(2)}) %collective-permute-start.7) | collective-permute-done | bytes 168992 | tf_op jit(solution)/shard_map/ppermute | solution.py:32
  369.4 3.8 collective-permute-done.8
  373.3 6.4 %collective-permute-start.13 = (f32[132,320]{1,0:T(8,128)S(1)}, f32[132,320]{1,0:T(8,128)S(1)}, u32[]{:S(2)}, u32[]{:S(2)}) collective-permute-start(f32[132,320]{1,0:T(8,128)S(1)} %get-tuple-element.55), channel_id=1, source_target_pairs={{0,28},{2,30},{4,24},{6,26},{8,20},{10,22},{12,16},{14,18},{16,12}... | collective-permute-start | bytes 506888 | tf_op jit(solution)/shard_map/ppermute | solution.py:32
  380.3 3.6 collective-permute-start.14
  384.7 4.2 collective-permute-done.10
  389.6 7.6 %collective-permute-done.11 = f32[132,320]{1,0:T(8,128)S(1)} collective-permute-done((f32[132,320]{1,0:T(8,128)S(1)}, f32[132,320]{1,0:T(8,128)S(1)}, u32[]{:S(2)}, u32[]{:S(2)}) %collective-permute-start.11) | collective-permute-done | bytes 168992 | tf_op jit(solution)/shard_map/ppermute | solution.py:32
  397.8 4.3 collective-permute-done.12
  402.9 3.0 collective-permute-done.13
  406.5 1.6 collective-permute-done.14
  408.8 4.4 gather_fusion.1
  413.2 4.3 copy.67
  417.5 4.7 reshape.130
  422.3 12.5 %reduce-scatter.2.cloned.1.call-done = f32[132,2560]{1,0:T(8,128)} async-done(((f32[132,5120]{1,0:T(8,128)}), f32[132,2560]{1,0:T(8,128)}) %reduce-scatter.2.cloned.1.call-update) | async-done | bytes 1351696 | tf_op jit(solution)/shard_map/reduce_scatter | solution.py:162
  434.8 1.5 add_convert_fusion
  436.3 31.5 %all-gather.3 = bf16[32,1,2560]{2,1,0:T(2,128)(2,1)S(1)} all-gather(bf16[1,1,2560]{2,1,0:T(2,128)(2,1)S(1)} %slice_bitcast_fusion), channel_id=1, replica_groups=mesh['seq'=16,'tp'=2] {'seq','tp'}, dimensions={0}, use_global_device_ids=true | all-gather | bytes 168960 | tf_op jit(solution)/shard_map/all_gather | solution.py:167
  468.9 1.8 all_gather.22
  470.9 19.8 %fusion.61 = (f32[20]{0:T(128)S(1)}, f32[20,4752]{1,0:T(8,128)S(1)}) fusion(bf16[5120,4752]{0,1:T(8,128)(2,1)} %param.29, f32[5120]{0:T(1024)S(1)} %convert_element_type.43, f32[20]{0:T(128)S(1)} %add_rsqrt_fusion, bf16[16,5120]{1,0:T(8,128)(2,1)S(1)} %reshape.131, bf16[4,5120]{1,0:T(4,128)(2,1)S(1)} %all_gather.22), kind=kOutput, calls=%fused_computation.118 | convolution fusion | flops 974021440 | bytes 49266080 | tf_op jit(solution)/shard_map/dot_general | solution.py:178
  491.5 49.9 %all-reduce.2 = (f32[640]{0:T(1024)S(1)}, f32[640]{0:T(1024)S(1)}) all-reduce(f32[640]{0:T(1024)S(1)} %dynamic-update-slice, f32[640]{0:T(1024)S(1)} %dynamic-update-slice.1), channel_id=2, replica_groups=mesh['seq'=16,'tp'=2] {'seq','tp'}, use_global_device_ids=true, to_apply=%add | all-reduce | flops 1280 | bytes 10240
  542.6 1.3 while.12
  (133 shorter events, 28.2 us)
Async XLA Ops:
  7.2 294.6 %copy-start = (bf16[2560,320]{0,1:T(8,128)(2,1)S(1)}, bf16[2560,320]{0,1:T(8,128)(2,1)}, u32[]{:S(2)}) copy-start(bf16[2560,320]{0,1:T(8,128)(2,1)} %param.27) | copy-start | bytes 4915204
  7.2 283.6 %all-gather.6.cloned.1.call-start = ((), (), s32[]{:S(2)}) async-start(), calls=%async_computation.2 | async-start | bytes 11837440 | tf_op jit(solution)/shard_map/all_gather | solution.py:159
  15.5 7.8 %copy-start.2 = (bf16[768,4,128]{2,0,1:T(8,128)(2,1)S(1)}, bf16[768,4,128]{2,0,1:T(8,128)(2,1)}, u32[]{:S(2)}) copy-start(bf16[768,4,128]{2,0,1:T(8,128)(2,1)} %copy.56) | copy-start | bytes 2359300
  23.3 7.4 %copy-start.3 = (bf16[1,1,768,512]{2,3,1,0:T(8,128)(2,1)S(1)}, bf16[1,1,768,512]{2,3,1,0:T(8,128)(2,1)}, u32[]{:S(2)}) copy-start(bf16[1,1,768,512]{2,3,1,0:T(8,128)(2,1)} %copy.52) | copy-start | bytes 2359300
  34.3 4.4 copy-start.7
  34.3 4.4 copy-start.10
  36.2 34.9 %copy-start.9 = (bf16[2,4,512]{2,1,0:T(4,128)(2,1)S(1)}, bf16[2,4,512]{2,1,0:T(4,128)(2,1)}, u32[]{:S(2)}) copy-start(bf16[2,4,512]{2,1,0:T(4,128)(2,1)} %param.23) | copy-start | bytes 24580
  147.5 287.3 %reduce-scatter.2.cloned.1.call-start = ((), (), s32[]{:S(2)}) async-start(), calls=%async_computation.1 | async-start | bytes 4177920 | tf_op jit(solution)/shard_map/reduce_scatter | solution.py:162
  319.2 9.6 %collective-permute-start = (f32[132,320]{1,0:T(8,128)S(1)}, f32[132,320]{1,0:T(8,128)S(1)}, u32[]{:S(2)}, u32[]{:S(2)}) collective-permute-start(f32[132,320]{1,0:T(8,128)S(1)} %get-tuple-element.68), channel_id=1, source_target_pairs={{0,2},{2,0},{4,6},{6,4},{8,10},{10,8},{12,14},{14,12},{16,18},{18,... | collective-permute-start | bytes 506888 | tf_op jit(solution)/shard_map/ppermute | solution.py:32
  319.9 11.5 %collective-permute-start.1 = (f32[132,320]{1,0:T(8,128)S(1)}, f32[132,320]{1,0:T(8,128)S(1)}, u32[]{:S(2)}, u32[]{:S(2)}) collective-permute-start(f32[132,320]{1,0:T(8,128)S(1)} %get-tuple-element.67), channel_id=1, source_target_pairs={{0,4},{2,6},{4,0},{6,2},{8,12},{10,14},{12,8},{14,10},{16,20},{18,... | collective-permute-start | bytes 506888 | tf_op jit(solution)/shard_map/ppermute | solution.py:32
  321.5 12.5 %collective-permute-start.2 = (f32[132,320]{1,0:T(8,128)S(1)}, f32[132,320]{1,0:T(8,128)S(1)}, u32[]{:S(2)}, u32[]{:S(2)}) collective-permute-start(f32[132,320]{1,0:T(8,128)S(1)} %get-tuple-element.66), channel_id=1, source_target_pairs={{0,6},{2,4},{4,2},{6,0},{8,14},{10,12},{12,10},{14,8},{16,22},{18,... | collective-permute-start | bytes 506888 | tf_op jit(solution)/shard_map/ppermute | solution.py:32
  322.7 14.2 %collective-permute-start.3 = (f32[132,320]{1,0:T(8,128)S(1)}, f32[132,320]{1,0:T(8,128)S(1)}, u32[]{:S(2)}, u32[]{:S(2)}) collective-permute-start(f32[132,320]{1,0:T(8,128)S(1)} %get-tuple-element.65), channel_id=1, source_target_pairs={{0,8},{2,10},{4,12},{6,14},{8,0},{10,2},{12,4},{14,6},{16,24},{18,... | collective-permute-start | bytes 506888 | tf_op jit(solution)/shard_map/ppermute | solution.py:32
  324.8 15.3 %collective-permute-start.4 = (f32[132,320]{1,0:T(8,128)S(1)}, f32[132,320]{1,0:T(8,128)S(1)}, u32[]{:S(2)}, u32[]{:S(2)}) collective-permute-start(f32[132,320]{1,0:T(8,128)S(1)} %get-tuple-element.64), channel_id=1, source_target_pairs={{0,10},{2,8},{4,14},{6,12},{8,2},{10,0},{12,6},{14,4},{16,26},{18,... | collective-permute-start | bytes 506888 | tf_op jit(solution)/shard_map/ppermute | solution.py:32
  328.8 17.7 %collective-permute-start.5 = (f32[132,320]{1,0:T(8,128)S(1)}, f32[132,320]{1,0:T(8,128)S(1)}, u32[]{:S(2)}, u32[]{:S(2)}) collective-permute-start(f32[132,320]{1,0:T(8,128)S(1)} %get-tuple-element.63), channel_id=1, source_target_pairs={{0,12},{2,14},{4,8},{6,10},{8,4},{10,6},{12,0},{14,2},{16,28},{18,... | collective-permute-start | bytes 506888 | tf_op jit(solution)/shard_map/ppermute | solution.py:32
  331.4 17.3 %collective-permute-start.6 = (f32[132,320]{1,0:T(8,128)S(1)}, f32[132,320]{1,0:T(8,128)S(1)}, u32[]{:S(2)}, u32[]{:S(2)}) collective-permute-start(f32[132,320]{1,0:T(8,128)S(1)} %get-tuple-element.62), channel_id=1, source_target_pairs={{0,14},{2,12},{4,10},{6,8},{8,6},{10,4},{12,2},{14,0},{16,30},{18,... | collective-permute-start | bytes 506888 | tf_op jit(solution)/shard_map/ppermute | solution.py:32
  334.0 34.7 %collective-permute-start.7 = (f32[132,320]{1,0:T(8,128)S(1)}, f32[132,320]{1,0:T(8,128)S(1)}, u32[]{:S(2)}, u32[]{:S(2)}) collective-permute-start(f32[132,320]{1,0:T(8,128)S(1)} %get-tuple-element.61), channel_id=1, source_target_pairs={{0,16},{2,18},{4,20},{6,22},{8,24},{10,26},{12,28},{14,30},{16,0},... | collective-permute-start | bytes 506888 | tf_op jit(solution)/shard_map/ppermute | solution.py:32
  336.9 36.3 %collective-permute-start.8 = (f32[132,320]{1,0:T(8,128)S(1)}, f32[132,320]{1,0:T(8,128)S(1)}, u32[]{:S(2)}, u32[]{:S(2)}) collective-permute-start(f32[132,320]{1,0:T(8,128)S(1)} %get-tuple-element.60), channel_id=1, source_target_pairs={{0,18},{2,16},{4,22},{6,20},{8,26},{10,24},{12,30},{14,28},{16,2},... | collective-permute-start | bytes 506888 | tf_op jit(solution)/shard_map/ppermute | solution.py:32
  340.1 40.3 %collective-permute-start.9 = (f32[132,320]{1,0:T(8,128)S(1)}, f32[132,320]{1,0:T(8,128)S(1)}, u32[]{:S(2)}, u32[]{:S(2)}) collective-permute-start(f32[132,320]{1,0:T(8,128)S(1)} %get-tuple-element.59), channel_id=1, source_target_pairs={{0,20},{2,22},{4,16},{6,18},{8,28},{10,30},{12,24},{14,26},{16,4},... | collective-permute-start | bytes 506888 | tf_op jit(solution)/shard_map/ppermute | solution.py:32
  346.5 42.4 %collective-permute-start.10 = (f32[132,320]{1,0:T(8,128)S(1)}, f32[132,320]{1,0:T(8,128)S(1)}, u32[]{:S(2)}, u32[]{:S(2)}) collective-permute-start(f32[132,320]{1,0:T(8,128)S(1)} %get-tuple-element.58), channel_id=1, source_target_pairs={{0,22},{2,20},{4,18},{6,16},{8,30},{10,28},{12,26},{14,24},{16,6},... | collective-permute-start | bytes 506888 | tf_op jit(solution)/shard_map/ppermute | solution.py:32
  348.7 48.4 %collective-permute-start.11 = (f32[132,320]{1,0:T(8,128)S(1)}, f32[132,320]{1,0:T(8,128)S(1)}, u32[]{:S(2)}, u32[]{:S(2)}) collective-permute-start(f32[132,320]{1,0:T(8,128)S(1)} %get-tuple-element.57), channel_id=1, source_target_pairs={{0,24},{2,26},{4,28},{6,30},{8,16},{10,18},{12,20},{14,22},{16,8},... | collective-permute-start | bytes 506888 | tf_op jit(solution)/shard_map/ppermute | solution.py:32
  368.7 33.5 %collective-permute-start.12 = (f32[132,320]{1,0:T(8,128)S(1)}, f32[132,320]{1,0:T(8,128)S(1)}, u32[]{:S(2)}, u32[]{:S(2)}) collective-permute-start(f32[132,320]{1,0:T(8,128)S(1)} %get-tuple-element.56), channel_id=1, source_target_pairs={{0,26},{2,24},{4,30},{6,28},{8,18},{10,16},{12,22},{14,20},{16,10}... | collective-permute-start | bytes 506888 | tf_op jit(solution)/shard_map/ppermute | solution.py:32
  373.3 32.6 %collective-permute-start.13 = (f32[132,320]{1,0:T(8,128)S(1)}, f32[132,320]{1,0:T(8,128)S(1)}, u32[]{:S(2)}, u32[]{:S(2)}) collective-permute-start(f32[132,320]{1,0:T(8,128)S(1)} %get-tuple-element.55), channel_id=1, source_target_pairs={{0,28},{2,30},{4,24},{6,26},{8,20},{10,22},{12,16},{14,18},{16,12}... | collective-permute-start | bytes 506888 | tf_op jit(solution)/shard_map/ppermute | solution.py:32
  380.3 27.8 %collective-permute-start.14 = (f32[132,320]{1,0:T(8,128)S(1)}, f32[132,320]{1,0:T(8,128)S(1)}, u32[]{:S(2)}, u32[]{:S(2)}) collective-permute-start(f32[132,320]{1,0:T(8,128)S(1)} %get-tuple-element.54), channel_id=1, source_target_pairs={{0,30},{2,28},{4,26},{6,24},{8,22},{10,20},{12,18},{14,16},{16,14}... | collective-permute-start | bytes 506888 | tf_op jit(solution)/shard_map/ppermute | solution.py:32
  417.5 4.8 copy-start.8
  417.5 17.3 %copy-start.4 = (bf16[128,2560]{1,0:T(8,128)(2,1)S(1)}, bf16[128,2560]{1,0:T(8,128)(2,1)}, u32[]{:S(2)}) copy-start(bf16[128,2560]{1,0:T(8,128)(2,1)} %param.16) | copy-start | bytes 1966084
  417.5 17.3 %copy-start.6 = (bf16[4,2560]{1,0:T(4,128)(2,1)S(1)}, bf16[4,2560]{1,0:T(4,128)(2,1)}, u32[]{:S(2)}) copy-start(bf16[4,2560]{1,0:T(4,128)(2,1)} %param.21) | copy-start | bytes 61444
  436.3 54.4 %copy-start.5 = (bf16[4,2560]{1,0:T(4,128)(2,1)}, bf16[4,2560]{1,0:T(4,128)(2,1)S(1)}, u32[]{:S(2)}) copy-start(bf16[4,2560]{1,0:T(4,128)(2,1)S(1)} %slice.72) | copy-start | bytes 61444
  470.9 73.9 %copy-start.1 = (bf16[2560,320]{0,1:T(8,128)(2,1)S(1)}, bf16[2560,320]{0,1:T(8,128)(2,1)}, u32[]{:S(2)}) copy-start(bf16[2560,320]{0,1:T(8,128)(2,1)} %param.27) | copy-start | bytes 4915204
Sparse Core Ops, SparseCore 0:
  147.6 143.1 all-gather.5
  422.4 12.3 reduce-scatter.1
